TPU v7x, 32 devices: a whole 2x2x4 slice. The times are simulated.
32 devices in a mesh: sta: 8 (over z, x), tm: 4 (over y, core).
Axes of the slice: x: 2, y: 2, z: 4, core: 2. Of those that a mesh axis runs over, the one named last changes fastest.
Arguments:
- records: float32 [16, 1, 65536], P('sta', None, 'tm'), may hold values from -6 to 6
- pair_blocks: int32 [24, 2], P('sta'), may hold values from 0 to 7, as said below
- pair_count: int32 [8], P('sta'), may hold values from 0 to 3, as said below
Outputs:
- correlations: float32 [24, 2, 2, 2048], P('sta', None, None, 'tm')
Inputs may be any that keep to these rules, and one draw needn't show every extreme that they name: `pair_blocks`: slot q belongs to owner o = q // 3. Every slot names blocks a <= b with o <= a and b <= o + 3, both below 8; the slots in use have a < b. `pair_count`: an owner with no higher block within 3 has no slot in use.
All inputs are finite; a program needn't handle non-finite values.
Results may differ from a plain program's by a relative error of at most 0.0003.
Values sent between devices are 32-bit elements; how exact they have to be, the bound alone decides.
No kernel may reach another device: no remote copies, remote signals or barrier semaphores. Data moves between devices by JAX's collectives and lax.ppermute only.
A program may use at most 64 MiB of HBM per device.

v0:
```python
import math
import jax
import jax.numpy as jnp
from jax import lax
from jax.sharding import PartitionSpec as P

SAMPLES = 65536
FACTOR_A = 256
BAND = 32
LAGS = 4
REACH = 3
highest = lax.Precision.HIGHEST
epsilon = 1e-06


def passed_along(block, axis, distance):
    devices = range(lax.axis_size(axis))
    route = [(i - distance, i) for i in devices if i - distance in devices]
    return lax.ppermute(block, axis, route)


def angles(row_ids, col_ids, modulus):
    product = row_ids[:, None] * col_ids[None, :] % modulus
    radians = product.astype(jnp.float32) * (2.0 * math.pi / modulus)
    return (jnp.cos(radians), jnp.sin(radians))


def matmul(left_mat, right_mat):
    return jnp.dot(left_mat, right_mat, precision=highest, preferred_element_type=jnp.float32)


def local(records, pair_blocks, pair_count):
    stations, hour_count, time_cols = records.shape
    time_devices = lax.axis_size("tm")
    time_rank = lax.axis_index("tm")
    owner_id = lax.axis_index("sta")
    factor_a = FACTOR_A
    factor_b = SAMPLES // FACTOR_A
    rows_local = factor_a // time_devices
    cols_local = factor_b // time_devices
    series = stations * hour_count
    arranged = records.reshape(series, rows_local, factor_b).transpose(1, 0, 2)
    spread = lax.all_to_all(arranged, "tm", split_axis=2, concat_axis=0, tiled=True)
    index_a = jnp.arange(factor_a, dtype=jnp.int32)
    index_b = jnp.arange(factor_b, dtype=jnp.int32)
    paired = rows_local == 2 * BAND and factor_a == 2 * BAND * time_devices
    if paired:
        owner_of_row = index_a // rows_local
        place_in_row = index_a % rows_local
        k1_order = jnp.where(
            place_in_row < BAND,
            BAND * owner_of_row + place_in_row,
            factor_a - BAND * (owner_of_row + 2) + place_in_row,
        )
        k1_ids = jnp.concatenate(
            [
                BAND * time_rank + jnp.arange(BAND, dtype=jnp.int32),
                factor_a - BAND * (time_rank + 1) + jnp.arange(BAND, dtype=jnp.int32),
            ]
        )
    else:
        k1_order = index_a
        k1_ids = time_rank * rows_local + jnp.arange(rows_local, dtype=jnp.int32)
    cosine_a, sine_a = angles(k1_order, index_a, factor_a)
    flat_rows = spread.reshape(factor_a, series * cols_local)
    both_a = jnp.concatenate([cosine_a, -sine_a], axis=0)
    section = matmul(both_a, flat_rows).reshape(2, factor_a, series, cols_local)
    section_real, section_imag = (section[0], section[1])
    col_global = time_rank * cols_local + jnp.arange(cols_local, dtype=jnp.int32)
    cosine_t, sine_t = angles(k1_order, col_global, SAMPLES)
    twisted_real = section_real * cosine_t[:, None, :] + section_imag * sine_t[:, None, :]
    twisted_imag = section_imag * cosine_t[:, None, :] - section_real * sine_t[:, None, :]
    twisted = jnp.stack([twisted_real, twisted_imag], axis=2)
    moved = lax.all_to_all(twisted, "tm", split_axis=0, concat_axis=3, tiled=True)
    cosine_b, sine_b = angles(index_b, index_b, factor_b)
    forward_b = jnp.concatenate(
        [jnp.concatenate([cosine_b, -sine_b], axis=1), jnp.concatenate([sine_b, cosine_b], axis=1)],
        axis=0,
    )
    spec = matmul(moved.reshape(rows_local * series, 2 * factor_b), forward_b)
    banded = spec.reshape(rows_local // BAND, BAND, series, 2, factor_b)
    band_power = jnp.mean(
        banded[:, :, :, 0] * banded[:, :, :, 0] + banded[:, :, :, 1] * banded[:, :, :, 1],
        axis=1,
        keepdims=True,
    )
    band_scale = lax.rsqrt(band_power + epsilon)
    whitened = (banded * band_scale[:, :, :, None]).reshape(rows_local, series, 2, factor_b)
    if paired:
        scale_row = band_scale[:, 0].transpose(1, 0, 2)[None]
        sent = jnp.concatenate(
            [spec.reshape(rows_local, series, 2, factor_b)[: BAND + 1], scale_row]
        )

        def rebuilt(piece):
            spec_part = piece[: BAND + 1]
            scale_low = piece[BAND + 1, :, 0][None, :, None, :]
            scale_high = piece[BAND + 1, :, 1][None, :, None, :]
            conj_sign = (1 - 2 * lax.iota(jnp.int32, 2)).astype(jnp.float32)[None, None, :, None]
            mirrored = spec_part[1:BAND][::-1, :, :, ::-1] * conj_sign
            high = jnp.concatenate([spec_part[BAND:], mirrored])
            return jnp.concatenate([spec_part[:BAND] * scale_low, high * scale_high])

    else:
        sent = whitened

        def rebuilt(piece):
            return piece

    pieces = [whitened]
    for distance in range(1, REACH + 1):
        pieces.append(rebuilt(passed_along(sent, "sta", -distance)))
    nearby = jnp.stack(pieces).reshape(REACH + 1, rows_local, stations, hour_count, 2, factor_b)
    slot_total = pair_blocks.shape[0]
    first_off = pair_blocks[:, 0] - owner_id
    second_off = pair_blocks[:, 1] - owner_id
    left_spec = jnp.stack(
        [
            lax.dynamic_index_in_dim(nearby, first_off[s], 0, keepdims=False)
            for s in range(slot_total)
        ]
    )
    right_spec = jnp.stack(
        [
            lax.dynamic_index_in_dim(nearby, second_off[s], 0, keepdims=False)
            for s in range(slot_total)
        ]
    )
    left_real = left_spec[:, :, :, None, :, 0]
    left_imag = left_spec[:, :, :, None, :, 1]
    right_real = right_spec[:, :, None, :, :, 0]
    right_imag = right_spec[:, :, None, :, :, 1]
    cross_real = jnp.sum(left_real * right_real + left_imag * right_imag, axis=4)
    cross_imag = jnp.sum(left_imag * right_real - left_real * right_imag, axis=4)
    cross = jnp.concatenate([cross_real, cross_imag], axis=-1)
    inverse_b = jnp.concatenate(
        [jnp.concatenate([cosine_b, sine_b], axis=1), jnp.concatenate([-sine_b, cosine_b], axis=1)],
        axis=0,
    )
    lag = matmul(cross.reshape(-1, 2 * factor_b), inverse_b).reshape(
        slot_total, rows_local, stations, stations, 2, factor_b
    )
    lag_real, lag_imag = (lag[:, :, :, :, 0], lag[:, :, :, :, 1])
    cosine_u, sine_u = angles(k1_ids, index_b, SAMPLES)
    turn_real = (
        lag_real * cosine_u[None, :, None, None, :] - lag_imag * sine_u[None, :, None, None, :]
    )
    turn_imag = (
        lag_real * sine_u[None, :, None, None, :] + lag_imag * cosine_u[None, :, None, None, :]
    )
    lag_ids = jnp.concatenate(
        [jnp.arange(LAGS, dtype=jnp.int32), factor_a - LAGS + jnp.arange(LAGS, dtype=jnp.int32)]
    )
    cosine_l, sine_l = angles(lag_ids, k1_ids, factor_a)
    lag_weights = jnp.concatenate([cosine_l, -sine_l], axis=1).reshape(
        time_devices, 2 * LAGS // time_devices, 2 * rows_local
    )
    turned = jnp.concatenate([turn_real, turn_imag], axis=1)
    scale_out = 1.0 / math.sqrt(SAMPLES * hour_count)
    live_mask = (jnp.arange(slot_total) < pair_count[0]).astype(jnp.float32) * scale_out
    lag_block = jnp.einsum(
        "dwp,spijm->dsijwm",
        lag_weights,
        turned,
        precision=highest,
        preferred_element_type=jnp.float32,
    )
    lag_block = lag_block * live_mask[None, :, None, None, None, None]
    gathered = lax.all_to_all(lag_block, "tm", split_axis=0, concat_axis=0, tiled=True)
    total = jnp.sum(gathered, axis=0)
    return total.reshape(slot_total, stations, stations, 2 * LAGS * factor_b // time_devices)


def solution(mesh):
    placed = (P("sta", None, "tm"), P("sta", None), P("sta"))
    return jax.shard_map(
        local, mesh=mesh, in_specs=placed, out_specs=P("sta", None, None, "tm"), check_vma=False
    )
```

profile of v0, /device:TPU:2, one launch (start us, length us, event | category | flops | bytes accessed | tf_op | source)
XLA Modules:
  0.0 73.7 jit_solution(5561566885266259954)
XLA Ops:
  0.0 1.3 %reduce.1 = f32[2,16384]{1,0:T(2,128)S(1)} reduce(f32[2,1,16384]{2,1,0:T(1,128)} %param.3, f32[]{:T(128)} %constant.136), dimensions={1}, to_apply=%param.3.reduce_sub_computation | reduce | bytes 262148 | tf_op args[0]
  1.5 0.9 %reshape.339 = f32[4,1,8192]{2,1,0:T(1,128)} reshape(f32[256,2,64]{2,1,0:T(2,128)S(1)} %bitcast.123) | data formatting | bytes 262144
  2.4 3.3 %all-to-all-start = ((f32[4,1,8192]{2,1,0:T(1,128)}), f32[4,1,8192]{2,1,0:T(1,128)S(1)}, u32[]{:S(2)}, u32[]{:S(2)}) async-start(f32[4,1,8192]{2,1,0:T(1,128)} %reshape.339), calls=%async_computation | async-start | bytes 262144 | tf_op jit(solution)/shard_map/all_to_all | solution.py:43
  5.7 1.0 %fusion.31 = (f32[256,256]{0,1:T(8,128)S(1)}, f32[256,256]{0,1:T(8,128)S(1)}) fusion(), kind=kLoop, calls=%fused_computation.80 | loop fusion | flops 917504 | bytes 524288 | tf_op jit(solution)/shard_map/sin | solution.py:25
  6.8 1.0 %fusion.35 = f32[256,256]{0,1:T(8,128)S(1)} fusion(), kind=kLoop, calls=%fused_computation.87 | loop fusion | flops 983040 | bytes 262144 | tf_op jit(solution)/shard_map/neg | solution.py:77
  7.8 0.7 fusion.66
  16.1 1.0 %fusion.33 = (f32[256,256]{0,1:T(8,128)S(1)}, f32[256,256]{0,1:T(8,128)S(1)}) fusion(s32[256]{0:T(256)S(1)} %compare_select_fusion.1), kind=kLoop, calls=%fused_computation.82 | loop fusion | flops 983040 | bytes 525312 | tf_op jit(solution)/shard_map/cos | solution.py:25
  22.5 0.5 broadcast.457
  23.1 1.0 %reduce.2 = f32[4,8192]{1,0:T(4,128)S(1)} reduce(f32[4,1,8192]{2,1,0:T(1,128)S(1)} %all-to-all-done, f32[]{:T(128)} %broadcast.457), dimensions={1}, to_apply=%all_to_all.25.reduce_sub_computation | reduce | bytes 262148 | tf_op jit(solution)/shard_map/all_to_all | solution.py:43
  25.7 1.3 %reshape.341 = f32[4,1,16384]{2,1,0:T(1,128)} reshape(f32[256,2,2,64]{3,2,1,0:T(2,128)S(1)} %copy.50) | data formatting | bytes 524288
  27.0 3.4 %all-to-all-start.1 = ((f32[4,1,16384]{2,1,0:T(1,128)}), f32[4,1,16384]{2,1,0:T(1,128)S(1)}, u32[]{:S(2)}, u32[]{:S(2)}) async-start(f32[4,1,16384]{2,1,0:T(1,128)} %reshape.341), calls=%async_computation.1 | async-start | bytes 524288 | tf_op jit(solution)/shard_map/all_to_all | solution.py:74
  30.5 5.8 %all-to-all-done.1 = f32[4,1,16384]{2,1,0:T(1,128)S(1)} async-done(((f32[4,1,16384]{2,1,0:T(1,128)}), f32[4,1,16384]{2,1,0:T(1,128)S(1)}, u32[]{:S(2)}, u32[]{:S(2)}) %all-to-all-start.1) | async-done | bytes 262176 | tf_op jit(solution)/shard_map/all_to_all | solution.py:74
  36.4 1.4 %reduce.3 = f32[4,16384]{1,0:T(4,128)S(1)} reduce(f32[4,1,16384]{2,1,0:T(1,128)S(1)} %all-to-all-done.1, f32[]{:T(128)} %broadcast.457), dimensions={1}, to_apply=%all_to_all.28.reduce_sub_computation | reduce | bytes 524292 | tf_op jit(solution)/shard_map/all_to_all | solution.py:74
  38.8 1.2 %fusion.9 = f32[128,512]{1,0:T(8,128)S(1)} fusion(f32[128,512]{1,0:T(8,128)S(1)} %reshape.330, f32[256,256]{0,1:T(8,128)S(1)} %get-tuple-element.54, f32[256,256]{0,1:T(8,128)S(1)} %get-tuple-element.53, f32[256,256]{0,1:T(8,128)S(1)} %fusion.35), kind=kOutput, calls=%fused_computation.15 | convolution fusion | flops 403439616 | bytes 1310720 | tf_op jit(solution)/shard_map/dot_general | solution.py:29
  40.7 1.9 %collective-permute-start = (f32[34,2,2,256]{3,0,2,1:T(8,128)S(1)}, f32[34,2,2,256]{3,0,2,1:T(8,128)S(1)}, u32[]{:S(2)}, u32[]{:S(2)}) collective-permute-start(f32[34,2,2,256]{3,0,2,1:T(8,128)S(1)} %pad_maximum_fusion.9), channel_id=1, source_target_pairs={{4,0},{8,4},{12,8},{16,12},{20,16},{24,20},{28,24},{5,1},{9,5},{13... | collective-permute-start | bytes 417800 | tf_op jit(solution)/shard_map/ppermute | solution.py:19
  42.6 1.3 %collective-permute-start.1 = (f32[34,2,2,256]{3,0,2,1:T(8,128)S(1)}, f32[34,2,2,256]{3,0,2,1:T(8,128)S(1)}, u32[]{:S(2)}, u32[]{:S(2)}) collective-permute-start(f32[34,2,2,256]{3,0,2,1:T(8,128)S(1)} %pad_maximum_fusion.9), channel_id=1, source_target_pairs={{8,0},{12,4},{16,8},{20,12},{24,16},{28,20},{9,1},{13,5},{17,9},{2... | collective-permute-start | bytes 417800 | tf_op jit(solution)/shard_map/ppermute | solution.py:19
  43.9 1.5 %collective-permute-start.2 = (f32[34,2,2,256]{3,0,2,1:T(8,128)S(1)}, f32[34,2,2,256]{3,0,2,1:T(8,128)S(1)}, u32[]{:S(2)}, u32[]{:S(2)}) collective-permute-start(f32[34,2,2,256]{3,0,2,1:T(8,128)S(1)} %pad_maximum_fusion.9), channel_id=1, source_target_pairs={{12,0},{16,4},{20,8},{24,12},{28,16},{13,1},{17,5},{21,9},{25,13},... | collective-permute-start | bytes 417800 | tf_op jit(solution)/shard_map/ppermute | solution.py:19
  45.6 4.9 %collective-permute-done = f32[34,2,2,256]{3,0,2,1:T(8,128)S(1)} collective-permute-done((f32[34,2,2,256]{3,0,2,1:T(8,128)S(1)}, f32[34,2,2,256]{3,0,2,1:T(8,128)S(1)}, u32[]{:S(2)}, u32[]{:S(2)}) %collective-permute-start) | collective-permute-done | bytes 139296 | tf_op jit(solution)/shard_map/ppermute | solution.py:19
  50.5 1.1 %collective-permute-done.1 = f32[34,2,2,256]{3,0,2,1:T(8,128)S(1)} collective-permute-done((f32[34,2,2,256]{3,0,2,1:T(8,128)S(1)}, f32[34,2,2,256]{3,0,2,1:T(8,128)S(1)}, u32[]{:S(2)}, u32[]{:S(2)}) %collective-permute-start.1) | collective-permute-done | bytes 139296 | tf_op jit(solution)/shard_map/ppermute | solution.py:19
  51.9 8.7 %collective-permute-done.2 = f32[34,2,2,256]{3,0,2,1:T(8,128)S(1)} collective-permute-done((f32[34,2,2,256]{3,0,2,1:T(8,128)S(1)}, f32[34,2,2,256]{3,0,2,1:T(8,128)S(1)}, u32[]{:S(2)}, u32[]{:S(2)}) %collective-permute-start.2) | collective-permute-done | bytes 139296 | tf_op jit(solution)/shard_map/ppermute | solution.py:19
  62.5 2.7 %fusion = f32[3,64,2,2,2,256]{5,1,4,3,2,0:T(8,128)S(1)} fusion(f32[2,256,512,1,1,1]{2,1,0,5,4,3:T(8,128)S(1)} %bitcast.120, f32[3,64,2,2,256]{4,1,3,2,0:T(8,128)S(1)} %get-tuple-element.8, f32[3,64,2,2,256]{4,1,3,2,0:T(8,128)S(1)} %get-tuple-element.7), kind=kOutput, calls=%fused_computation.1 | convolution fusion | flops 2416312320 | bytes 4194304 | tf_op jit(solution)/shard_map/dot_general | solution.py:29
  65.4 0.9 %fusion.7 = f32[4,3,2,2,2,256]{5,0,4,3,2,1:T(4,128)S(1)} fusion(f32[3,64,2,2,256]{4,1,3,2,0:T(8,128)S(1)} %get-tuple-element.6, f32[3,64,2,2,256]{4,1,3,2,0:T(8,128)S(1)} %get-tuple-element.5, f32[3]{0:T(128)S(1)} %compare_select_fusion, f32[4,2,64]{2,0,1:T(4,128)S(1)} %get-tuple-element.32, f32[4,2,64]{2,0,1:T(4,128)S(1)} %get-tuple-element.31), kind=kOutput, calls=%fused_computation.13 | convolution fusion | flops 38167552 | bytes 1675276 | tf_op jit(solution)/shard_map/dwp,spijm->dsijwm/dot_general | solution.py:161
  66.4 6.7 %all_to_all.35 = f32[4,3,2,2,2,256]{5,4,3,2,1,0:T(2,128)S(1)} all-to-all(f32[4,3,2,2,2,256]{5,4,3,2,1,0:T(2,128)S(1)} %copy.58), channel_id=1, replica_groups=mesh['sta'=8,'tm'=4] {'tm'}, dimensions={0} | all-to-all | bytes 196608 | tf_op jit(solution)/shard_map/all_to_all | solution.py:169
  73.1 0.6 reshape.333
  (80 shorter events, 7.0 us)
Async XLA Ops:
  0.0 7.8 %copy-start = (s32[3,2]{0,1:T(2,128)S(1)}, s32[3,2]{0,1:T(2,128)}, u32[]{:S(2)}) copy-start(s32[3,2]{0,1:T(2,128)} %param.4) | copy-start | bytes 76
  2.4 20.2 %all-to-all-start = ((f32[4,1,8192]{2,1,0:T(1,128)}), f32[4,1,8192]{2,1,0:T(1,128)S(1)}, u32[]{:S(2)}, u32[]{:S(2)}) async-start(f32[4,1,8192]{2,1,0:T(1,128)} %reshape.339), calls=%async_computation | async-start | bytes 262144 | tf_op jit(solution)/shard_map/all_to_all | solution.py:43
  27.0 9.4 %all-to-all-start.1 = ((f32[4,1,16384]{2,1,0:T(1,128)}), f32[4,1,16384]{2,1,0:T(1,128)S(1)}, u32[]{:S(2)}, u32[]{:S(2)}) async-start(f32[4,1,16384]{2,1,0:T(1,128)} %reshape.341), calls=%async_computation.1 | async-start | bytes 524288 | tf_op jit(solution)/shard_map/all_to_all | solution.py:74
  40.7 9.9 %collective-permute-start = (f32[34,2,2,256]{3,0,2,1:T(8,128)S(1)}, f32[34,2,2,256]{3,0,2,1:T(8,128)S(1)}, u32[]{:S(2)}, u32[]{:S(2)}) collective-permute-start(f32[34,2,2,256]{3,0,2,1:T(8,128)S(1)} %pad_maximum_fusion.9), channel_id=1, source_target_pairs={{4,0},{8,4},{12,8},{16,12},{20,16},{24,20},{28,24},{5,1},{9,5},{13... | collective-permute-start | bytes 417800 | tf_op jit(solution)/shard_map/ppermute | solution.py:19
  42.6 9.0 %collective-permute-start.1 = (f32[34,2,2,256]{3,0,2,1:T(8,128)S(1)}, f32[34,2,2,256]{3,0,2,1:T(8,128)S(1)}, u32[]{:S(2)}, u32[]{:S(2)}) collective-permute-start(f32[34,2,2,256]{3,0,2,1:T(8,128)S(1)} %pad_maximum_fusion.9), channel_id=1, source_target_pairs={{8,0},{12,4},{16,8},{20,12},{24,16},{28,20},{9,1},{13,5},{17,9},{2... | collective-permute-start | bytes 417800 | tf_op jit(solution)/shard_map/ppermute | solution.py:19
  43.9 16.7 %collective-permute-start.2 = (f32[34,2,2,256]{3,0,2,1:T(8,128)S(1)}, f32[34,2,2,256]{3,0,2,1:T(8,128)S(1)}, u32[]{:S(2)}, u32[]{:S(2)}) collective-permute-start(f32[34,2,2,256]{3,0,2,1:T(8,128)S(1)} %pad_maximum_fusion.9), channel_id=1, source_target_pairs={{12,0},{16,4},{20,8},{24,12},{28,16},{13,1},{17,5},{21,9},{25,13},... | collective-permute-start | bytes 417800 | tf_op jit(solution)/shard_map/ppermute | solution.py:19
where the time goes:
time: 74.3 us; the launch traced here: 73.7 us
  waiting for transfers between devices  20.5 us (28%)
  between operations  12.6 us (17%)
  starting transfers between devices  11.4 us (15%)
  other arithmetic  9.12 us (12%)
  local copies, waits for them, and re-layouts  8.13 us (11%)
  blocking collectives  6.67 us (9%)
  matrix products  5.25 us (7%)
    ppermute x3, waiting for transfers between devices, passed_along(): return lax.ppermute(block, axis, route)  14.7 us
    all_to_all x1, blocking collectives, local(): lax.all_to_all(lag_block, 'tm', split_axis=0, concat_axis=0, tiled=True)  6.67 us
    all_to_all x1, waiting for transfers between devices, local(): lax.all_to_all(twisted, 'tm', split_axis=0, concat_axis=3, tiled=True)  5.84 us
    ppermute x3, starting transfers between devices, passed_along(): return lax.ppermute(block, axis, route)  4.69 us
    dot_general x3, matrix products, matmul(): jnp.dot(left_mat, right_mat, precision=highest, preferred_element_type=jn...  4.32 us
    all_to_all x1, starting transfers between devices, local(): lax.all_to_all(twisted, 'tm', split_axis=0, concat_axis=3, tiled=True)  3.4 us
    all_to_all x1, starting transfers between devices, local(): lax.all_to_all(arranged, 'tm', split_axis=2, concat_axis=0, tiled=True)  3.32 us
    unnamed x13, local copies, waits for them, and re-layouts  2.85 us
  transfers between devices with their start and end apart: 5, of which 4 were waited for; matrix products, arithmetic and copies ran while one was open for 7% of the time, Pallas kernels for 0%

commit v1 on v0

--- a/solution.py
+++ b/solution.py
@@ -11,6 +11,28 @@
 REACH = 3
 highest = lax.Precision.HIGHEST
 epsilon = 1e-06
+
+
+def split_up(x, dim, size):
+    before, after = (x.shape[:dim], x.shape[dim + 1 :])
+    return jnp.moveaxis(x.reshape(*before, size, -1, *after), dim, 0)
+
+
+def in_order(blocks, dim):
+    blocks = jnp.moveaxis(blocks, 0, dim)
+    shape = blocks.shape
+    return blocks.reshape(*shape[:dim], shape[dim] * shape[dim + 1], *shape[dim + 2 :])
+
+
+def exchange_in_pairs(array, axis, split_dim, concat_dim):
+    devices, index = (lax.axis_size(axis), lax.axis_index(axis))
+    tiles = split_up(array, split_dim, devices)
+    finished = [tiles[index]]
+    for turn in range(1, devices):
+        sent = tiles[index ^ turn]
+        finished.append(lax.ppermute(sent, axis, [(i, i ^ turn) for i in range(devices)]))
+    tiles = jnp.stack(finished)[index ^ jnp.arange(devices)]
+    return in_order(tiles, concat_dim)
 
 
 def passed_along(block, axis, distance):
@@ -40,7 +62,7 @@
     cols_local = factor_b // time_devices
     series = stations * hour_count
     arranged = records.reshape(series, rows_local, factor_b).transpose(1, 0, 2)
-    spread = lax.all_to_all(arranged, "tm", split_axis=2, concat_axis=0, tiled=True)
+    spread = exchange_in_pairs(arranged, "tm", 2, 0)
     index_a = jnp.arange(factor_a, dtype=jnp.int32)
     index_b = jnp.arange(factor_b, dtype=jnp.int32)
     paired = rows_local == 2 * BAND and factor_a == 2 * BAND * time_devices

time: 74.3 us -> 71.5 us (0.962)
  starting transfers between devices: 11.4 us -> 10.3 us
  other arithmetic: 9.12 us -> 8.17 us
    all_to_all x1 -> x0, starting transfers between devices: 3.32 us -> none  [local(): lax.all_to_all(arranged, 'tm', split_axis=2, concat_axis=0, tiled=True)]
    ppermute x0 -> x3, starting transfers between devices: none -> 1.92 us  [exchange_in_pairs(): lax.ppermute(sent, axis, [(i, i ^ turn) for i in range(devices)])]
    unnamed x13 -> x11, local copies, waits for them, and re-layouts: 2.85 us -> 1.71 us
    all_to_all x1 -> x0, other arithmetic: 0.98 us -> none  [local(): lax.all_to_all(arranged, 'tm', split_axis=2, concat_axis=0, tiled=True)]
    all_to_all x3 -> x0, local copies, waits for them, and re-layouts: 0.88 us -> none  [local(): lax.all_to_all(arranged, 'tm', split_axis=2, concat_axis=0, tiled=True)]
    gather x0 -> x2, local copies, waits for them, and re-layouts: none -> 0.77 us  [exchange_in_pairs(): tiles = jnp.stack(finished)[index ^ jnp.arange(devices)]]
  transfers between devices with their start and end apart: 5 -> 7, of which waited for: 4 -> 4; matrix products, arithmetic and copies ran while one was open for 7% -> 7% of each run, Pallas kernels for 0% -> 0%
where the time goes in v1:
time: 71.5 us; the launch traced here: 71.1 us
  waiting for transfers between devices  20.4 us (29%)
  between operations  12.6 us (18%)
  starting transfers between devices  10.3 us (14%)
  other arithmetic  8.17 us (11%)
  local copies, waits for them, and re-layouts  7.61 us (11%)
  blocking collectives  6.67 us (9%)
  matrix products  5.25 us (7%)
    ppermute x3, waiting for transfers between devices, passed_along(): return lax.ppermute(block, axis, route)  14.6 us
    all_to_all x1, blocking collectives, local(): lax.all_to_all(lag_block, 'tm', split_axis=0, concat_axis=0, tiled=True)  6.67 us
    all_to_all x1, waiting for transfers between devices, local(): lax.all_to_all(twisted, 'tm', split_axis=0, concat_axis=3, tiled=True)  5.84 us
    ppermute x3, starting transfers between devices, passed_along(): return lax.ppermute(block, axis, route)  4.98 us
    dot_general x3, matrix products, matmul(): jnp.dot(left_mat, right_mat, precision=highest, preferred_element_type=jn...  4.32 us
    all_to_all x1, starting transfers between devices, local(): lax.all_to_all(twisted, 'tm', split_axis=0, concat_axis=3, tiled=True)  3.4 us
    ppermute x3, starting transfers between devices, exchange_in_pairs(): lax.ppermute(sent, axis, [(i, i ^ turn) for i in range(devices)])  1.92 us
    cos x4, other arithmetic, angles(): return (jnp.cos(radians), jnp.sin(radians))  1.85 us
  transfers between devices with their start and end apart: 7, of which 4 were waited for; matrix products, arithmetic and copies ran while one was open for 7% of the time, Pallas kernels for 0%

profile of v1, /device:TPU:2, one launch (start us, length us, event | category | flops | bytes accessed | tf_op | source)
XLA Modules:
  0.0 71.1 jit_solution(10604396756739040704)
XLA Ops:
  0.0 1.3 %reduce.1 = f32[2,16384]{1,0:T(2,128)S(1)} reduce(f32[2,1,16384]{2,1,0:T(1,128)} %param.3, f32[]{:T(128)} %constant.143), dimensions={1}, to_apply=%param.3.reduce_sub_computation | reduce | bytes 262148 | tf_op args[0]
  1.8 1.6 %collective-permute-start.1 = (f32[64,2,64]{2,0,1:T(8,128)S(1)}, f32[64,2,64]{2,0,1:T(8,128)S(1)}, u32[]{:S(2)}, u32[]{:S(2)}) collective-permute-start(f32[64,2,64]{2,0,1:T(8,128)S(1)} %bitcast.137), channel_id=1, source_target_pairs={{0,2},{1,3},{2,0},{3,1},{4,6},{5,7},{6,4},{7,5},{8,10},{9,11},{10,... | collective-permute-start | bytes 98312 | tf_op jit(solution)/shard_map/ppermute | solution.py:33
  3.7 1.0 %fusion.31 = (f32[256,256]{0,1:T(8,128)S(1)}, f32[256,256]{0,1:T(8,128)S(1)}) fusion(), kind=kLoop, calls=%fused_computation.82 | loop fusion | flops 917504 | bytes 524288 | tf_op jit(solution)/shard_map/sin | solution.py:47
  4.7 1.0 %fusion.35 = f32[256,256]{0,1:T(8,128)S(1)} fusion(), kind=kLoop, calls=%fused_computation.89 | loop fusion | flops 983040 | bytes 262144 | tf_op jit(solution)/shard_map/neg | solution.py:99
  5.7 1.0 %fusion.33 = (f32[256,256]{0,1:T(8,128)S(1)}, f32[256,256]{0,1:T(8,128)S(1)}) fusion(s32[256]{0:T(256)S(1)} %compare_select_fusion.2), kind=kLoop, calls=%fused_computation.84 | loop fusion | flops 983040 | bytes 525312 | tf_op jit(solution)/shard_map/cos | solution.py:47
  8.3 0.7 fusion.67
  20.5 0.6 gather_fusion
  21.5 0.5 fusion.14
  22.4 1.2 %reshape.369 = f32[4,1,16384]{2,1,0:T(1,128)} reshape(f32[256,2,2,64]{3,2,1,0:T(2,128)S(1)} %copy.41) | data formatting | bytes 524288
  23.6 3.4 %all-to-all-start = ((f32[4,1,16384]{2,1,0:T(1,128)}), f32[4,1,16384]{2,1,0:T(1,128)S(1)}, u32[]{:S(2)}, u32[]{:S(2)}) async-start(f32[4,1,16384]{2,1,0:T(1,128)} %reshape.369), calls=%async_computation | async-start | bytes 524288 | tf_op jit(solution)/shard_map/all_to_all | solution.py:96
  27.2 5.8 %all-to-all-done = f32[4,1,16384]{2,1,0:T(1,128)S(1)} async-done(((f32[4,1,16384]{2,1,0:T(1,128)}), f32[4,1,16384]{2,1,0:T(1,128)S(1)}, u32[]{:S(2)}, u32[]{:S(2)}) %all-to-all-start) | async-done | bytes 262176 | tf_op jit(solution)/shard_map/all_to_all | solution.py:96
  33.0 0.5 broadcast.492
  33.5 1.4 %reduce.2 = f32[4,16384]{1,0:T(4,128)S(1)} reduce(f32[4,1,16384]{2,1,0:T(1,128)S(1)} %all-to-all-done, f32[]{:T(128)} %broadcast.492), dimensions={1}, to_apply=%all_to_all.14.reduce_sub_computation | reduce | bytes 524292 | tf_op jit(solution)/shard_map/all_to_all | solution.py:96
  36.0 1.2 %fusion.9 = f32[128,512]{1,0:T(8,128)S(1)} fusion(f32[128,512]{1,0:T(8,128)S(1)} %reshape.352, f32[256,256]{0,1:T(8,128)S(1)} %get-tuple-element.58, f32[256,256]{0,1:T(8,128)S(1)} %get-tuple-element.57, f32[256,256]{0,1:T(8,128)S(1)} %fusion.35), kind=kOutput, calls=%fused_computation.16 | convolution fusion | flops 403439616 | bytes 1310720 | tf_op jit(solution)/shard_map/dot_general | solution.py:51
  38.0 2.2 %collective-permute-start.3 = (f32[34,2,2,256]{3,0,2,1:T(8,128)S(1)}, f32[34,2,2,256]{3,0,2,1:T(8,128)S(1)}, u32[]{:S(2)}, u32[]{:S(2)}) collective-permute-start(f32[34,2,2,256]{3,0,2,1:T(8,128)S(1)} %pad_maximum_fusion.10), channel_id=1, source_target_pairs={{4,0},{8,4},{12,8},{16,12},{20,16},{24,20},{28,24},{5,1},{9,5},{13... | collective-permute-start | bytes 417800 | tf_op jit(solution)/shard_map/ppermute | solution.py:41
  40.2 1.3 %collective-permute-start.4 = (f32[34,2,2,256]{3,0,2,1:T(8,128)S(1)}, f32[34,2,2,256]{3,0,2,1:T(8,128)S(1)}, u32[]{:S(2)}, u32[]{:S(2)}) collective-permute-start(f32[34,2,2,256]{3,0,2,1:T(8,128)S(1)} %pad_maximum_fusion.10), channel_id=1, source_target_pairs={{8,0},{12,4},{16,8},{20,12},{24,16},{28,20},{9,1},{13,5},{17,9},{2... | collective-permute-start | bytes 417800 | tf_op jit(solution)/shard_map/ppermute | solution.py:41
  41.5 1.5 %collective-permute-start.5 = (f32[34,2,2,256]{3,0,2,1:T(8,128)S(1)}, f32[34,2,2,256]{3,0,2,1:T(8,128)S(1)}, u32[]{:S(2)}, u32[]{:S(2)}) collective-permute-start(f32[34,2,2,256]{3,0,2,1:T(8,128)S(1)} %pad_maximum_fusion.10), channel_id=1, source_target_pairs={{12,0},{16,4},{20,8},{24,12},{28,16},{13,1},{17,5},{21,9},{25,13},... | collective-permute-start | bytes 417800 | tf_op jit(solution)/shard_map/ppermute | solution.py:41
  43.1 4.8 %collective-permute-done.3 = f32[34,2,2,256]{3,0,2,1:T(8,128)S(1)} collective-permute-done((f32[34,2,2,256]{3,0,2,1:T(8,128)S(1)}, f32[34,2,2,256]{3,0,2,1:T(8,128)S(1)}, u32[]{:S(2)}, u32[]{:S(2)}) %collective-permute-start.3) | collective-permute-done | bytes 139296 | tf_op jit(solution)/shard_map/ppermute | solution.py:41
  47.9 1.3 %collective-permute-done.4 = f32[34,2,2,256]{3,0,2,1:T(8,128)S(1)} collective-permute-done((f32[34,2,2,256]{3,0,2,1:T(8,128)S(1)}, f32[34,2,2,256]{3,0,2,1:T(8,128)S(1)}, u32[]{:S(2)}, u32[]{:S(2)}) %collective-permute-start.4) | collective-permute-done | bytes 139296 | tf_op jit(solution)/shard_map/ppermute | solution.py:41
  49.4 8.6 %collective-permute-done.5 = f32[34,2,2,256]{3,0,2,1:T(8,128)S(1)} collective-permute-done((f32[34,2,2,256]{3,0,2,1:T(8,128)S(1)}, f32[34,2,2,256]{3,0,2,1:T(8,128)S(1)}, u32[]{:S(2)}, u32[]{:S(2)}) %collective-permute-start.5) | collective-permute-done | bytes 139296 | tf_op jit(solution)/shard_map/ppermute | solution.py:41
  59.8 2.7 %fusion = f32[3,64,2,2,2,256]{5,1,4,3,2,0:T(8,128)S(1)} fusion(f32[2,256,512,1,1,1]{2,1,0,5,4,3:T(8,128)S(1)} %bitcast.127, f32[3,64,2,2,256]{4,1,3,2,0:T(8,128)S(1)} %get-tuple-element.8, f32[3,64,2,2,256]{4,1,3,2,0:T(8,128)S(1)} %get-tuple-element.7), kind=kOutput, calls=%fused_computation.2 | convolution fusion | flops 2416312320 | bytes 4194304 | tf_op jit(solution)/shard_map/dot_general | solution.py:51
  62.7 0.9 %fusion.7 = f32[4,3,2,2,2,256]{5,0,4,3,2,1:T(4,128)S(1)} fusion(f32[3,64,2,2,256]{4,1,3,2,0:T(8,128)S(1)} %get-tuple-element.6, f32[3,64,2,2,256]{4,1,3,2,0:T(8,128)S(1)} %get-tuple-element.5, f32[3]{0:T(128)S(1)} %compare_select_fusion.1, f32[4,2,64]{2,0,1:T(4,128)S(1)} %get-tuple-element.36, f32[4,2,64]{2,0,1:T(4,128)S(1)} %get-tuple-element.35), kind=kOutput, calls=%fused_computation.14 | convolution fusion | flops 38167552 | bytes 1675276 | tf_op jit(solution)/shard_map/dwp,spijm->dsijwm/dot_general | solution.py:183
  63.7 6.7 %all_to_all.20 = f32[4,3,2,2,2,256]{5,4,3,2,1,0:T(2,128)S(1)} all-to-all(f32[4,3,2,2,2,256]{5,4,3,2,1,0:T(2,128)S(1)} %copy.49), channel_id=1, replica_groups=mesh['sta'=8,'tm'=4] {'tm'}, dimensions={0} | all-to-all | bytes 196608 | tf_op jit(solution)/shard_map/all_to_all | solution.py:191
  70.4 0.6 reshape.355
  (85 shorter events, 6.8 us)
Async XLA Ops:
  0.0 8.2 %copy-start = (s32[3,2]{0,1:T(2,128)S(1)}, s32[3,2]{0,1:T(2,128)}, u32[]{:S(2)}) copy-start(s32[3,2]{0,1:T(2,128)} %param.4) | copy-start | bytes 76
  1.7 18.7 %collective-permute-start = (f32[64,2,64]{2,0,1:T(8,128)S(1)}, f32[64,2,64]{2,0,1:T(8,128)S(1)}, u32[]{:S(2)}, u32[]{:S(2)}) collective-permute-start(f32[64,2,64]{2,0,1:T(8,128)S(1)} %bitcast.139), channel_id=1, source_target_pairs={{0,1},{1,0},{2,3},{3,2},{4,5},{5,4},{6,7},{7,6},{8,9},{9,8},{10,11... | collective-permute-start | bytes 98312 | tf_op jit(solution)/shard_map/ppermute | solution.py:33
  1.8 18.6 %collective-permute-start.1 = (f32[64,2,64]{2,0,1:T(8,128)S(1)}, f32[64,2,64]{2,0,1:T(8,128)S(1)}, u32[]{:S(2)}, u32[]{:S(2)}) collective-permute-start(f32[64,2,64]{2,0,1:T(8,128)S(1)} %bitcast.137), channel_id=1, source_target_pairs={{0,2},{1,3},{2,0},{3,1},{4,6},{5,7},{6,4},{7,5},{8,10},{9,11},{10,... | collective-permute-start | bytes 98312 | tf_op jit(solution)/shard_map/ppermute | solution.py:33
  3.4 17.1 %collective-permute-start.2 = (f32[64,2,64]{2,0,1:T(8,128)S(1)}, f32[64,2,64]{2,0,1:T(8,128)S(1)}, u32[]{:S(2)}, u32[]{:S(2)}) collective-permute-start(f32[64,2,64]{2,0,1:T(8,128)S(1)} %bitcast.136), channel_id=1, source_target_pairs={{0,3},{1,2},{2,1},{3,0},{4,7},{5,6},{6,5},{7,4},{8,11},{9,10},{10,... | collective-permute-start | bytes 98312 | tf_op jit(solution)/shard_map/ppermute | solution.py:33
  23.6 9.4 %all-to-all-start = ((f32[4,1,16384]{2,1,0:T(1,128)}), f32[4,1,16384]{2,1,0:T(1,128)S(1)}, u32[]{:S(2)}, u32[]{:S(2)}) async-start(f32[4,1,16384]{2,1,0:T(1,128)} %reshape.369), calls=%async_computation | async-start | bytes 524288 | tf_op jit(solution)/shard_map/all_to_all | solution.py:96
  38.0 9.9 %collective-permute-start.3 = (f32[34,2,2,256]{3,0,2,1:T(8,128)S(1)}, f32[34,2,2,256]{3,0,2,1:T(8,128)S(1)}, u32[]{:S(2)}, u32[]{:S(2)}) collective-permute-start(f32[34,2,2,256]{3,0,2,1:T(8,128)S(1)} %pad_maximum_fusion.10), channel_id=1, source_target_pairs={{4,0},{8,4},{12,8},{16,12},{20,16},{24,20},{28,24},{5,1},{9,5},{13... | collective-permute-start | bytes 417800 | tf_op jit(solution)/shard_map/ppermute | solution.py:41
  40.2 8.9 %collective-permute-start.4 = (f32[34,2,2,256]{3,0,2,1:T(8,128)S(1)}, f32[34,2,2,256]{3,0,2,1:T(8,128)S(1)}, u32[]{:S(2)}, u32[]{:S(2)}) collective-permute-start(f32[34,2,2,256]{3,0,2,1:T(8,128)S(1)} %pad_maximum_fusion.10), channel_id=1, source_target_pairs={{8,0},{12,4},{16,8},{20,12},{24,16},{28,20},{9,1},{13,5},{17,9},{2... | collective-permute-start | bytes 417800 | tf_op jit(solution)/shard_map/ppermute | solution.py:41
  41.5 16.5 %collective-permute-start.5 = (f32[34,2,2,256]{3,0,2,1:T(8,128)S(1)}, f32[34,2,2,256]{3,0,2,1:T(8,128)S(1)}, u32[]{:S(2)}, u32[]{:S(2)}) collective-permute-start(f32[34,2,2,256]{3,0,2,1:T(8,128)S(1)} %pad_maximum_fusion.10), channel_id=1, source_target_pairs={{12,0},{16,4},{20,8},{24,12},{28,16},{13,1},{17,5},{21,9},{25,13},... | collective-permute-start | bytes 417800 | tf_op jit(solution)/shard_map/ppermute | solution.py:41
